TPU v7x, 32 devices: a whole 2x2x4 slice. The times are simulated.
32 devices in a mesh: gz: 4 (over z), xy: 8 (over y, x, core).
Axes of the slice: x: 2, y: 2, z: 4, core: 2. Of those that a mesh axis runs over, the one named last changes fastest.
Arguments:
- tile_image: bfloat16 [4, 8, 4, 4, 2, 128], P('gz', 'xy'), may hold values from -6 to 6
- tile_target: bfloat16 [4, 8, 4, 3, 4, 2, 128], P('gz', 'xy'), may hold values from 0 to 1
- owner_counts: int32 [4, 8], P('gz', 'xy'), may hold values from 0 to 4, as said below
- tile_list: int32 [4, 8, 4], P('gz', 'xy'), may hold values from -1 to 15, as said below
- w_in: bfloat16 [27, 32], replicated, may hold values from -1.25 to 1.25
- w_res: bfloat16 [27, 32, 32], replicated, may hold values from -0.21875 to 0.21875
- w_down: bfloat16 [8, 64, 32], replicated, may hold values from -0.375 to 0.375
- w_mid: bfloat16 [27, 64, 64], replicated, may hold values from -0.15625 to 0.15625
- w_up: bfloat16 [8, 32, 64], replicated, may hold values from -0.75 to 0.75
- head_weight: bfloat16 [3, 32], replicated, may hold values from -1 to 1
Outputs:
- err_tiles: bfloat16 [4, 8, 4, 3, 4, 2, 128], P('gz', 'xy')
- grad_in: float32 [27, 32], replicated
- grad_res: float32 [27, 32, 32], replicated
- grad_down: float32 [8, 64, 32], replicated
- grad_mid: float32 [27, 64, 64], replicated
- grad_up: float32 [8, 32, 64], replicated
- head_weight_gradient: float32 [3, 32], replicated
Inputs may be any that keep to these rules, and one draw needn't show every extreme that they name: `owner_counts`: in each depth row the counts add up to 16, and some owner of every row holds exactly 4 tiles. `tile_list`: in each depth row the live slots (s < owner_counts) name every position 0 to 15 exactly once; the other slots hold -1.
All inputs are finite; a program needn't handle non-finite values.
Results may differ from a plain program's by a relative error of at most 0.0046.
Values may be sent and summed in bfloat16 or wider, within the bound.
No kernel may reach another device: no remote copies, remote signals or barrier semaphores. Data moves between devices by JAX's collectives and lax.ppermute only.
A program may use at most 64 MiB of HBM per device.

v0:
```python
import jax
import jax.numpy as jnp
from jax import lax
from jax.sharding import PartitionSpec as P

TPD = 2


def with_halo(cells, sides, width):
    for axis, dim in sides:
        count = lax.axis_size(axis)
        ends = count - 1
        head = lax.slice_in_dim(cells, 0, width, axis=dim)
        tail = lax.slice_in_dim(cells, cells.shape[dim] - width, cells.shape[dim], axis=dim)
        cells = jnp.concatenate(
            [
                lax.ppermute(tail, axis, [(i, (i + 1) % count) for i in range(ends)]),
                cells,
                lax.ppermute(head, axis, [((i + 1) % count, i) for i in range(ends)]),
            ],
            axis=dim,
        )
    return cells


def framed(field):
    padded = with_halo(field, (("gz", 1), ("xy", 3)), 1)
    return jnp.pad(padded, ((0, 0), (0, 0), (1, 1), (0, 0)))


def convolve(padded, weights):
    depth = padded.shape[1] - 2
    height = padded.shape[2] - 2
    width = padded.shape[3] - 2
    total = None
    for tap in range(27):
        off_z, off_y, off_x = (tap // 9, tap // 3 % 3, tap % 3)
        window = padded[:, off_z : off_z + depth, off_y : off_y + height, off_x : off_x + width]
        term = jnp.einsum("oc,czyx->ozyx", weights[tap], window, preferred_element_type=jnp.float32)
        total = term if total is None else total + term
    return total


def tap_grads(grad, padded):
    depth, height, width = grad.shape[1:]
    terms = []
    for tap in range(27):
        off_z, off_y, off_x = (tap // 9, tap // 3 % 3, tap % 3)
        window = padded[:, off_z : off_z + depth, off_y : off_y + height, off_x : off_x + width]
        terms.append(jnp.einsum("ozyx,czyx->oc", grad, window, preferred_element_type=jnp.float32))
    return jnp.stack(terms)


def flipped(weights):
    return jnp.transpose(weights[::-1], (0, 2, 1))


def strided(field, tap):
    return field[:, tap // 4 :: 2, tap // 2 % 2 :: 2, tap % 2 :: 2]


def alternate(parts):
    chans, depth, height, width = parts.shape[1:]
    return (
        parts.reshape(2, 2, 2, chans, depth, height, width)
        .transpose(3, 4, 0, 5, 1, 6, 2)
        .reshape(chans, 2 * depth, 2 * height, 2 * width)
    )


def local(
    tile_image, tile_target, owner_counts, tile_list, w_in, w_res, w_down, w_mid, w_up, head_weight
):
    single_float = jnp.float32
    brain_float_half = jnp.bfloat16
    ranks = lax.axis_size("xy")
    layers = lax.axis_size("gz")
    column = lax.axis_index("xy")
    slots = tile_list.shape[2]
    depth, height, width = (tile_image.shape[3], tile_image.shape[4], tile_image.shape[5])
    per_dev = TPD
    total_tiles = ranks * per_dev
    slot_list = tile_list[0, 0]
    live = jnp.arange(slots) < owner_counts[0, 0]
    select = ((slot_list[None, :] == jnp.arange(total_tiles)[:, None]) & live[None, :]).astype(
        brain_float_half
    )
    wanted = column * per_dev + jnp.arange(per_dev)
    piece_img = lax.all_gather(tile_image, "xy", axis=1, tiled=True)
    piece_tgt = lax.all_gather(tile_target, "xy", axis=1, tiled=True)
    piece_cnt = lax.all_gather(owner_counts, "xy", axis=1, tiled=True)
    piece_list = lax.all_gather(tile_list, "xy", axis=1, tiled=True)
    owners = piece_list.shape[1]
    piece_live = jnp.arange(slots)[None, :] < piece_cnt[0][:, None]
    match = ((piece_list[0][:, :, None] == wanted[None, None, :]) & piece_live[:, :, None]).astype(
        brain_float_half
    )
    acc_img = jnp.einsum(
        "kst,kszyx->tzyx", match, piece_img[0], preferred_element_type=single_float
    )
    acc_tgt = jnp.einsum(
        "kst,ksazyx->tazyx", match, piece_tgt[0], preferred_element_type=single_float
    )
    rows_hit = (jnp.arange(ranks)[:, None] == jnp.arange(owners)[None, :]).astype(single_float)
    acc_hit = jnp.dot(rows_hit, jnp.sum(match.astype(single_float), axis=1))
    acc_img, acc_tgt, acc_hit = (acc_img, acc_tgt, acc_hit)
    mine_img = acc_img.astype(brain_float_half)
    mine_tgt = acc_tgt.astype(brain_float_half)
    owner_hit = acc_hit.astype(brain_float_half)
    image = mine_img.transpose(1, 2, 0, 3).reshape(1, depth, height, per_dev * width)
    target = mine_tgt.transpose(1, 2, 3, 0, 4).reshape(3, depth, height, per_dev * width)
    voxel_cells = depth * height * per_dev * width * ranks * layers
    image_pad = framed(image)
    h0 = jax.nn.relu(convolve(image_pad, w_in[:, :, None])).astype(brain_float_half)
    h0_pad = framed(h0)
    h1 = jax.nn.relu(h0.astype(single_float) + convolve(h0_pad, w_res)).astype(brain_float_half)
    down_sum = None
    for tap in range(8):
        term = jnp.einsum(
            "oc,czyx->ozyx", w_down[tap], strided(h1, tap), preferred_element_type=single_float
        )
        down_sum = term if down_sum is None else down_sum + term
    dfield = jax.nn.relu(down_sum).astype(brain_float_half)
    dfield_pad = framed(dfield)
    cfield = jax.nn.relu(dfield.astype(single_float) + convolve(dfield_pad, w_mid)).astype(
        brain_float_half
    )
    upward = alternate(
        jnp.stack(
            [
                jnp.einsum("oc,czyx->ozyx", w_up[tap], cfield, preferred_element_type=single_float)
                for tap in range(8)
            ]
        )
    )
    signal_field = jax.nn.relu(h1.astype(single_float) + upward).astype(brain_float_half)
    logits = jnp.einsum(
        "ac,czyx->azyx", head_weight, signal_field, preferred_element_type=single_float
    )
    affinity_map = jax.nn.sigmoid(logits)
    error_field = affinity_map - target.astype(single_float)
    err_out = error_field.astype(brain_float_half)
    err_local = err_out.reshape(3, depth, height, per_dev, width).transpose(3, 0, 1, 2, 4)
    sending = owner_hit[:, :, None, None, None, None] * err_local[None]
    returned = lax.all_to_all(sending, "xy", split_axis=0, concat_axis=0, tiled=True)
    returned = returned.reshape((total_tiles, 3, depth, height, width))
    err_tiles = jnp.einsum(
        "ps,pazyx->sazyx", select, returned, preferred_element_type=single_float
    ).astype(brain_float_half)[None, None]
    logit_gradient = (error_field * affinity_map * (1.0 - affinity_map) / voxel_cells).astype(
        brain_float_half
    )
    head_weight_gradient = jnp.einsum(
        "mtnq,btnq->mb", logit_gradient, signal_field, preferred_element_type=single_float
    )
    gradient_total = jnp.einsum(
        "jn,jbrq->nbrq", head_weight, logit_gradient, preferred_element_type=single_float
    )
    gsf = jnp.where(signal_field > 0, gradient_total, 0.0).astype(brain_float_half)
    grad_up = jnp.stack(
        [
            jnp.einsum(
                "ozyx,czyx->oc", strided(gsf, tap), cfield, preferred_element_type=single_float
            )
            for tap in range(8)
        ]
    )
    gcoarse = None
    for tap in range(8):
        term = jnp.einsum(
            "oc,ozyx->czyx", w_up[tap], strided(gsf, tap), preferred_element_type=single_float
        )
        gcoarse = term if gcoarse is None else gcoarse + term
    gquad = jnp.where(cfield > 0, gcoarse, 0.0).astype(brain_float_half)
    grad_mid = tap_grads(gquad, dfield_pad)
    gdown = gquad.astype(single_float) + convolve(framed(gquad), flipped(w_mid))
    gdd = jnp.where(dfield > 0, gdown, 0.0).astype(brain_float_half)
    grad_down = jnp.stack(
        [
            jnp.einsum("ozyx,czyx->oc", gdd, strided(h1, tap), preferred_element_type=single_float)
            for tap in range(8)
        ]
    )
    spread = alternate(
        jnp.stack(
            [
                jnp.einsum("oc,ozyx->czyx", w_down[tap], gdd, preferred_element_type=single_float)
                for tap in range(8)
            ]
        )
    )
    gres = jnp.where(h1 > 0, gsf.astype(single_float) + spread, 0.0).astype(brain_float_half)
    grad_res = tap_grads(gres, h0_pad)
    gfirst = gres.astype(single_float) + convolve(framed(gres), flipped(w_res))
    gact = jnp.where(h0 > 0, gfirst, 0.0).astype(brain_float_half)
    grad_in = tap_grads(gact, image_pad)[:, :, 0]
    summed = lax.psum(
        (grad_in, grad_res, grad_down, grad_mid, grad_up, head_weight_gradient), ("gz", "xy")
    )
    return (err_tiles, summed[0], summed[1], summed[2], summed[3], summed[4], summed[5])


def solution(mesh):
    return jax.shard_map(
        local,
        mesh=mesh,
        in_specs=(
            P("gz", "xy", None, None, None, None),
            P("gz", "xy", None, None, None, None, None),
            P("gz", "xy"),
            P("gz", "xy", None),
            P(),
            P(),
            P(),
            P(),
            P(),
            P(),
        ),
        out_specs=(P("gz", "xy", None, None, None, None, None), P(), P(), P(), P(), P(), P()),
        check_vma=False,
    )
```

profile of v0, /device:TPU:0, one launch (start us, length us, event | category | flops | bytes accessed | tf_op | source)
XLA Modules:
  0.0 325.3 jit_solution(603947522372132895)
XLA Ops:
  7.8 1.2 dynamic-slice
  9.8 9.5 %all-reduce.3 = s32[8]{0:T(128)S(1)} all-reduce(s32[8]{0:T(128)S(1)} %bitcast_dynamic-update-slice_fusion), channel_id=1, replica_groups=mesh['gz'=4,'xy'=8] {'xy'}, use_global_device_ids=true, to_apply=%add.3 | all-reduce | flops 8 | bytes 64
  19.3 8.1 %all_gather.12 = s32[1,8,4]{2,0,1:T(1,128)S(1)} all-gather(s32[1,1,4]{2,0,1:T(1,128)} %bitcast.2102), channel_id=1, replica_groups=mesh['gz'=4,'xy'=8] {'xy'}, dimensions={1}, use_global_device_ids=true | all-gather | bytes 144 | tf_op jit(solution)/shard_map/all_gather | solution.py:92
  28.2 8.9 %all_gather.14 = bf16[1,8,4,4,2,128]{5,3,4,2,0,1:T(4,128)(2,1)S(1)} all-gather(bf16[1,1,4,4,2,128]{5,3,4,2,0,1:T(4,128)(2,1)S(1)} %copy.229), channel_id=1, replica_groups=mesh['gz'=4,'xy'=8] {'xy'}, dimensions={1}, use_global_device_ids=true | all-gather | bytes 73728 | tf_op jit(solution)/shard_map/all_gather | solution.py:89
  37.4 3.5 %collective-permute-start = (bf16[1,1,2,256]{3,2,1,0:T(2,128)(2,1)S(1)}, bf16[1,1,2,256]{3,2,1,0:T(2,128)(2,1)S(1)}, u32[]{:S(2)}, u32[]{:S(2)}) collective-permute-start(bf16[1,1,2,256]{3,2,1,0:T(2,128)(2,1)S(1)} %get-tuple-element.194), channel_id=1, source_target_pairs={{0,8},{8,16},{16,24},{1,9},{9,17},{17,25},{2,10},{10,18},{18,26},{... | collective-permute-start | bytes 3080 | tf_op jit(solution)/shard_map/ppermute | solution.py:17
  40.9 1.3 collective-permute-start.1
  42.2 1.0 bitcast_convert_fusion.52
  43.2 0.9 bitcast_convert_fusion.51
  44.1 0.8 fusion.359
  45.0 0.8 fusion.350
  45.8 0.9 fusion.340
  46.7 1.3 copy.240
  50.6 8.6 %all_gather.15 = bf16[1,8,4,3,4,2,128]{6,4,5,3,2,0,1:T(4,128)(2,1)S(1)} all-gather(bf16[1,1,4,3,4,2,128]{6,4,5,3,2,0,1:T(4,128)(2,1)S(1)} %copy.234), channel_id=1, replica_groups=mesh['gz'=4,'xy'=8] {'xy'}, dimensions={1}, use_global_device_ids=true | all-gather | bytes 221184 | tf_op jit(solution)/shard_map/all_gather | solution.py:90
  63.3 2.2 collective-permute-start.2
  65.5 1.3 collective-permute-start.3
  66.8 2.2 collective-permute-done.3
  69.1 0.8 slice_bitcast_fusion.108
  71.3 4.5 %collective-permute-start.4 = (bf16[32,1,2,256]{3,0,2,1:T(8,128)(2,1)S(1)}, bf16[32,1,2,256]{3,0,2,1:T(8,128)(2,1)S(1)}, u32[]{:S(2)}, u32[]{:S(2)}) collective-permute-start(bf16[32,1,2,256]{3,0,2,1:T(8,128)(2,1)S(1)} %get-tuple-element.91), channel_id=1, source_target_pairs={{0,8},{8,16},{16,24},{1,9},{9,17},{17,25},{2,10},{10,18},{18,26},{... | collective-permute-start | bytes 98312 | tf_op jit(solution)/shard_map/ppermute | solution.py:17
  75.9 1.3 collective-permute-start.5
  77.5 4.2 %collective-permute-done.5 = bf16[32,1,2,256]{3,0,2,1:T(8,128)(2,1)S(1)} collective-permute-done((bf16[32,1,2,256]{3,0,2,1:T(8,128)(2,1)S(1)}, bf16[32,1,2,256]{3,0,2,1:T(8,128)(2,1)S(1)}, u32[]{:S(2)}, u32[]{:S(2)}) %collective-permute-start.5) | collective-permute-done | bytes 32800 | tf_op jit(solution)/shard_map/ppermute | solution.py:19
  81.8 2.8 collective-permute-start.6
  84.7 1.3 collective-permute-start.7
  86.2 2.6 collective-permute-done.7
  100.7 1.9 fusion.751
  102.6 1.0 fusion.752
  105.3 3.5 %collective-permute-start.8 = (bf16[64,1,1,128]{3,0,1,2:T(8,128)(2,1)S(1)}, bf16[64,1,1,128]{3,0,1,2:T(8,128)(2,1)S(1)}, u32[]{:S(2)}, u32[]{:S(2)}) collective-permute-start(bf16[64,1,1,128]{3,0,1,2:T(8,128)(2,1)S(1)} %get-tuple-element.101), channel_id=1, source_target_pairs={{0,8},{8,16},{16,24},{1,9},{9,17},{17,25},{2,10},{10,18},{18,26},{... | collective-permute-start | bytes 49160 | tf_op jit(solution)/shard_map/ppermute | solution.py:17
  108.8 1.3 collective-permute-start.9
  110.2 4.2 %collective-permute-done.9 = bf16[64,1,1,128]{3,0,1,2:T(8,128)(2,1)S(1)} collective-permute-done((bf16[64,1,1,128]{3,0,1,2:T(8,128)(2,1)S(1)}, bf16[64,1,1,128]{3,0,1,2:T(8,128)(2,1)S(1)}, u32[]{:S(2)}, u32[]{:S(2)}) %collective-permute-start.9) | collective-permute-done | bytes 16416 | tf_op jit(solution)/shard_map/ppermute | solution.py:19
  114.6 3.7 %collective-permute-start.10 = (bf16[64,4,1,1]{3,0,1,2:T(8,128)(2,1)S(1)}, bf16[64,4,1,1]{3,0,1,2:T(8,128)(2,1)S(1)}, u32[]{:S(2)}, u32[]{:S(2)}) collective-permute-start(bf16[64,4,1,1]{3,0,1,2:T(8,128)(2,1)S(1)} %get-tuple-element.95), channel_id=1, source_target_pairs={{0,1},{1,2},{2,3},{3,4},{4,5},{5,6},{6,7},{8,9},{9,10},{10,11},{11... | collective-permute-start | bytes 1544 | tf_op jit(solution)/shard_map/ppermute | solution.py:17
  118.3 1.5 collective-permute-start.11
  119.9 2.4 collective-permute-done.11
  138.8 3.5 %collective-permute-start.12 = (bf16[64,1,1,128]{3,0,1,2:T(8,128)(2,1)S(1)}, bf16[64,1,1,128]{3,0,1,2:T(8,128)(2,1)S(1)}, u32[]{:S(2)}, u32[]{:S(2)}) collective-permute-start(bf16[64,1,1,128]{3,0,1,2:T(8,128)(2,1)S(1)} %get-tuple-element.99), channel_id=1, source_target_pairs={{0,8},{8,16},{16,24},{1,9},{9,17},{17,25},{2,10},{10,18},{18,26},{... | collective-permute-start | bytes 49160 | tf_op jit(solution)/shard_map/ppermute | solution.py:17
  142.3 1.3 collective-permute-start.13
  143.6 0.8 broadcast_multiply_fusion
  144.4 7.7 %all-to-all-start = ((bf16[8,2,3,4,2,128]{5,1,4,3,2,0:T(2,128)(2,1)}), bf16[8,2,3,4,2,128]{5,1,4,3,2,0:T(2,128)(2,1)S(1)}, u32[]{:S(2)}, u32[]{:S(2)}) async-start(bf16[8,2,3,4,2,128]{5,1,4,3,2,0:T(2,128)(2,1)} %broadcast_multiply_fusion), calls=%async_computation | async-start | bytes 196608 | tf_op jit(solution)/shard_map/all_to_all | solution.py:145
  152.3 1.3 collective-permute-start.15
  153.6 3.0 collective-permute-start.14
  167.8 4.3 %collective-permute-start.16 = (bf16[32,1,2,256]{3,0,2,1:T(8,128)(2,1)S(1)}, bf16[32,1,2,256]{3,0,2,1:T(8,128)(2,1)S(1)}, u32[]{:S(2)}, u32[]{:S(2)}) collective-permute-start(bf16[32,1,2,256]{3,0,2,1:T(8,128)(2,1)S(1)} %get-tuple-element.81), channel_id=1, source_target_pairs={{0,8},{8,16},{16,24},{1,9},{9,17},{17,25},{2,10},{10,18},{18,26},{... | collective-permute-start | bytes 98312 | tf_op jit(solution)/shard_map/ppermute | solution.py:17
  172.1 1.3 collective-permute-start.17
  175.1 2.8 collective-permute-done.17
  178.0 2.6 collective-permute-start.18
  180.7 1.3 collective-permute-start.19
  182.1 5.0 %collective-permute-done.19 = bf16[32,6,2,1]{3,0,2,1:T(8,128)(2,1)S(1)} collective-permute-done((bf16[32,6,2,1]{3,0,2,1:T(8,128)(2,1)S(1)}, bf16[32,6,2,1]{3,0,2,1:T(8,128)(2,1)S(1)}, u32[]{:S(2)}, u32[]{:S(2)}) %collective-permute-start.19) | collective-permute-done | bytes 800 | tf_op jit(solution)/shard_map/ppermute | solution.py:19
  197.3 44.9 %all-reduce.4 = (f32[27,32]{1,0:T(8,128)}, f32[3,32]{1,0:T(4,128)}) all-reduce(f32[27,32]{1,0:T(8,128)S(1)} %bitcast.2093, f32[3,32]{1,0:T(4,128)S(1)} %copy-done.95), channel_id=1, replica_groups=mesh['gz'=4,'xy'=8] {'gz','xy'}, use_global_device_ids=true, to_apply=%region_1.2 | all-reduce | flops 960 | bytes 7680 | tf_op jit(solution)/shard_map/psum | solution.py:197
  243.1 70.2 %all-reduce.8.cloned.1.call-done = (f32[27,32,32]{2,1,0:T(8,128)}, f32[8,64,32]{1,2,0:T(8,128)}, f32[27,64,64]{2,1,0:T(8,128)}, f32[8,32,64]{2,1,0:T(8,128)}) async-done(((f32[27,32,32]{2,1,0:T(8,128)}, f32[8,64,32]{1,2,0:T(8,128)}, f32[27,64,64]{2,1,0:T(8,128)}, f32[8,32,64]{2,1,0:T(8,128)}), (f32[27,32,32]{2,1,0:T(8,128)}, f32[8,64,32]{1,2,0:T(8,128)}, f32[27,64,64]{2,1,0:T(8,128)}, ...) | async-done | bytes 684048 | tf_op jit(solution)/shard_map/psum | solution.py:197
  313.4 1.9 copy.810
  315.3 1.6 copy.811
  316.9 0.9 copy.812
  (528 shorter events, 64.4 us)
Async XLA Ops:
  7.2 119.9 %copy-start = (bf16[3,32]{1,0:T(4,128)(2,1)S(1)}, bf16[3,32]{1,0:T(4,128)(2,1)}, u32[]{:S(2)}) copy-start(bf16[3,32]{1,0:T(4,128)(2,1)} %param.19) | copy-start | bytes 580
  37.4 25.2 %collective-permute-start = (bf16[1,1,2,256]{3,2,1,0:T(2,128)(2,1)S(1)}, bf16[1,1,2,256]{3,2,1,0:T(2,128)(2,1)S(1)}, u32[]{:S(2)}, u32[]{:S(2)}) collective-permute-start(bf16[1,1,2,256]{3,2,1,0:T(2,128)(2,1)S(1)} %get-tuple-element.194), channel_id=1, source_target_pairs={{0,8},{8,16},{16,24},{1,9},{9,17},{17,25},{2,10},{10,18},{18,26},{... | collective-permute-start | bytes 3080 | tf_op jit(solution)/shard_map/ppermute | solution.py:17
  40.9 21.7 %collective-permute-start.1 = (bf16[1,1,2,256]{3,2,1,0:T(2,128)(2,1)S(1)}, bf16[1,1,2,256]{3,2,1,0:T(2,128)(2,1)S(1)}, u32[]{:S(2)}, u32[]{:S(2)}) collective-permute-start(bf16[1,1,2,256]{3,2,1,0:T(2,128)(2,1)S(1)} %get-tuple-element.193), channel_id=1, source_target_pairs={{8,0},{16,8},{24,16},{9,1},{17,9},{25,17},{10,2},{18,10},{26,18},{... | collective-permute-start | bytes 3080 | tf_op jit(solution)/shard_map/ppermute | solution.py:19
  45.8 4.0 %copy-start.1 = (bf16[27,64,64]{2,1,0:T(8,128)(2,1)S(1)}, bf16[27,64,64]{2,1,0:T(8,128)(2,1)}, u32[]{:S(2)}) copy-start(bf16[27,64,64]{2,1,0:T(8,128)(2,1)} %param.17) | copy-start | bytes 663556
  48.0 12.4 %copy-start.4 = (bf16[27,32,32]{2,1,0:T(8,128)(2,1)S(1)}, bf16[27,32,32]{2,1,0:T(8,128)(2,1)}, u32[]{:S(2)}) copy-start(bf16[27,32,32]{2,1,0:T(8,128)(2,1)} %param.15) | copy-start | bytes 165892
  63.3 3.6 %collective-permute-start.2 = (bf16[1,6,2,1]{3,2,1,0:T(2,128)(2,1)S(1)}, bf16[1,6,2,1]{3,2,1,0:T(2,128)(2,1)S(1)}, u32[]{:S(2)}, u32[]{:S(2)}) collective-permute-start(bf16[1,6,2,1]{3,2,1,0:T(2,128)(2,1)S(1)} %get-tuple-element.184), channel_id=1, source_target_pairs={{0,1},{1,2},{2,3},{3,4},{4,5},{5,6},{6,7},{8,9},{9,10},{10,11},{11... | collective-permute-start | bytes 80 | tf_op jit(solution)/shard_map/ppermute | solution.py:17
  65.5 3.5 %collective-permute-start.3 = (bf16[1,6,2,1]{3,2,1,0:T(2,128)(2,1)S(1)}, bf16[1,6,2,1]{3,2,1,0:T(2,128)(2,1)S(1)}, u32[]{:S(2)}, u32[]{:S(2)}) collective-permute-start(bf16[1,6,2,1]{3,2,1,0:T(2,128)(2,1)S(1)} %get-tuple-element.185), channel_id=1, source_target_pairs={{1,0},{2,1},{3,2},{4,3},{5,4},{6,5},{7,6},{9,8},{10,9},{11,10},{12... | collective-permute-start | bytes 80 | tf_op jit(solution)/shard_map/ppermute | solution.py:19
  71.3 6.1 %collective-permute-start.4 = (bf16[32,1,2,256]{3,0,2,1:T(8,128)(2,1)S(1)}, bf16[32,1,2,256]{3,0,2,1:T(8,128)(2,1)S(1)}, u32[]{:S(2)}, u32[]{:S(2)}) collective-permute-start(bf16[32,1,2,256]{3,0,2,1:T(8,128)(2,1)S(1)} %get-tuple-element.91), channel_id=1, source_target_pairs={{0,8},{8,16},{16,24},{1,9},{9,17},{17,25},{2,10},{10,18},{18,26},{... | collective-permute-start | bytes 98312 | tf_op jit(solution)/shard_map/ppermute | solution.py:17
  75.9 5.8 %collective-permute-start.5 = (bf16[32,1,2,256]{3,0,2,1:T(8,128)(2,1)S(1)}, bf16[32,1,2,256]{3,0,2,1:T(8,128)(2,1)S(1)}, u32[]{:S(2)}, u32[]{:S(2)}) collective-permute-start(bf16[32,1,2,256]{3,0,2,1:T(8,128)(2,1)S(1)} %get-tuple-element.92), channel_id=1, source_target_pairs={{8,0},{16,8},{24,16},{9,1},{17,9},{25,17},{10,2},{18,10},{26,18},{... | collective-permute-start | bytes 98312 | tf_op jit(solution)/shard_map/ppermute | solution.py:19
  81.8 4.4 %collective-permute-start.6 = (bf16[32,6,2,1]{3,0,2,1:T(8,128)(2,1)S(1)}, bf16[32,6,2,1]{3,0,2,1:T(8,128)(2,1)S(1)}, u32[]{:S(2)}, u32[]{:S(2)}) collective-permute-start(bf16[32,6,2,1]{3,0,2,1:T(8,128)(2,1)S(1)} %get-tuple-element.79), channel_id=1, source_target_pairs={{0,1},{1,2},{2,3},{3,4},{4,5},{5,6},{6,7},{8,9},{9,10},{10,11},{11... | collective-permute-start | bytes 2312 | tf_op jit(solution)/shard_map/ppermute | solution.py:17
  84.7 4.2 %collective-permute-start.7 = (bf16[32,6,2,1]{3,0,2,1:T(8,128)(2,1)S(1)}, bf16[32,6,2,1]{3,0,2,1:T(8,128)(2,1)S(1)}, u32[]{:S(2)}, u32[]{:S(2)}) collective-permute-start(bf16[32,6,2,1]{3,0,2,1:T(8,128)(2,1)S(1)} %get-tuple-element.80), channel_id=1, source_target_pairs={{1,0},{2,1},{3,2},{4,3},{5,4},{6,5},{7,6},{9,8},{10,9},{11,10},{12... | collective-permute-start | bytes 2312 | tf_op jit(solution)/shard_map/ppermute | solution.py:19
  86.0 7.8 %copy-start.5 = (bf16[32,4,2,256]{3,0,2,1:T(8,128)(2,1)}, bf16[32,4,2,256]{3,0,2,1:T(8,128)(2,1)S(1)}, u32[]{:S(2)}) copy-start(bf16[32,4,2,256]{3,0,2,1:T(8,128)(2,1)S(1)} %get-tuple-element.89) | copy-start | bytes 393220
  95.4 8.2 %copy-start.39 = (bf16[32,2,1,128]{3,0,2,1:T(8,128)(2,1)}, bf16[32,2,1,128]{3,0,2,1:T(8,128)(2,1)S(1)}, u32[]{:S(2)}) copy-start(bf16[32,2,1,128]{3,0,2,1:T(8,128)(2,1)S(1)} %slice.1254) | copy-start | bytes 49156
  96.1 7.7 %copy-start.37 = (bf16[32,2,1,128]{3,0,2,1:T(8,128)(2,1)}, bf16[32,2,1,128]{3,0,2,1:T(8,128)(2,1)S(1)}, u32[]{:S(2)}) copy-start(bf16[32,2,1,128]{3,0,2,1:T(8,128)(2,1)S(1)} %slice.1256) | copy-start | bytes 49156
  96.9 7.1 %copy-start.35 = (bf16[32,2,1,128]{3,0,2,1:T(8,128)(2,1)}, bf16[32,2,1,128]{3,0,2,1:T(8,128)(2,1)S(1)}, u32[]{:S(2)}) copy-start(bf16[32,2,1,128]{3,0,2,1:T(8,128)(2,1)S(1)} %slice.1258) | copy-start | bytes 49156
  97.6 6.6 %copy-start.33 = (bf16[32,2,1,128]{3,0,2,1:T(8,128)(2,1)}, bf16[32,2,1,128]{3,0,2,1:T(8,128)(2,1)S(1)}, u32[]{:S(2)}) copy-start(bf16[32,2,1,128]{3,0,2,1:T(8,128)(2,1)S(1)} %slice.1260) | copy-start | bytes 49156
  98.4 6.1 %copy-start.31 = (bf16[32,2,1,128]{3,0,2,1:T(8,128)(2,1)}, bf16[32,2,1,128]{3,0,2,1:T(8,128)(2,1)S(1)}, u32[]{:S(2)}) copy-start(bf16[32,2,1,128]{3,0,2,1:T(8,128)(2,1)S(1)} %slice.1262) | copy-start | bytes 49156
  99.1 5.5 %copy-start.29 = (bf16[32,2,1,128]{3,0,2,1:T(8,128)(2,1)}, bf16[32,2,1,128]{3,0,2,1:T(8,128)(2,1)S(1)}, u32[]{:S(2)}) copy-start(bf16[32,2,1,128]{3,0,2,1:T(8,128)(2,1)S(1)} %slice.1264) | copy-start | bytes 49156
  99.9 5.0 %copy-start.27 = (bf16[32,2,1,128]{3,0,2,1:T(8,128)(2,1)}, bf16[32,2,1,128]{3,0,2,1:T(8,128)(2,1)S(1)}, u32[]{:S(2)}) copy-start(bf16[32,2,1,128]{3,0,2,1:T(8,128)(2,1)S(1)} %slice.1266) | copy-start | bytes 49156
  100.6 4.4 %copy-start.25 = (bf16[32,2,1,128]{3,0,2,1:T(8,128)(2,1)}, bf16[32,2,1,128]{3,0,2,1:T(8,128)(2,1)S(1)}, u32[]{:S(2)}) copy-start(bf16[32,2,1,128]{3,0,2,1:T(8,128)(2,1)S(1)} %slice.1268) | copy-start | bytes 49156
  104.2 18.4 %copy-start.20 = (f32[2,128,64]{1,2,0:T(8,128)S(1)}, f32[2,128,64]{1,2,0:T(8,128)}, u32[]{:S(2)}) copy-start(f32[2,128,64]{1,2,0:T(8,128)} %convolution_add_fusion.42) | copy-start | bytes 196612
  105.3 4.9 %collective-permute-start.8 = (bf16[64,1,1,128]{3,0,1,2:T(8,128)(2,1)S(1)}, bf16[64,1,1,128]{3,0,1,2:T(8,128)(2,1)S(1)}, u32[]{:S(2)}, u32[]{:S(2)}) collective-permute-start(bf16[64,1,1,128]{3,0,1,2:T(8,128)(2,1)S(1)} %get-tuple-element.101), channel_id=1, source_target_pairs={{0,8},{8,16},{16,24},{1,9},{9,17},{17,25},{2,10},{10,18},{18,26},{... | collective-permute-start | bytes 49160 | tf_op jit(solution)/shard_map/ppermute | solution.py:17
  108.8 5.6 %collective-permute-start.9 = (bf16[64,1,1,128]{3,0,1,2:T(8,128)(2,1)S(1)}, bf16[64,1,1,128]{3,0,1,2:T(8,128)(2,1)S(1)}, u32[]{:S(2)}, u32[]{:S(2)}) collective-permute-start(bf16[64,1,1,128]{3,0,1,2:T(8,128)(2,1)S(1)} %get-tuple-element.102), channel_id=1, source_target_pairs={{8,0},{16,8},{24,16},{9,1},{17,9},{25,17},{10,2},{18,10},{26,18},{... | collective-permute-start | bytes 49160 | tf_op jit(solution)/shard_map/ppermute | solution.py:19
  114.6 8.0 %collective-permute-start.10 = (bf16[64,4,1,1]{3,0,1,2:T(8,128)(2,1)S(1)}, bf16[64,4,1,1]{3,0,1,2:T(8,128)(2,1)S(1)}, u32[]{:S(2)}, u32[]{:S(2)}) collective-permute-start(bf16[64,4,1,1]{3,0,1,2:T(8,128)(2,1)S(1)} %get-tuple-element.95), channel_id=1, source_target_pairs={{0,1},{1,2},{2,3},{3,4},{4,5},{5,6},{6,7},{8,9},{9,10},{10,11},{11... | collective-permute-start | bytes 1544 | tf_op jit(solution)/shard_map/ppermute | solution.py:17
  118.3 4.0 %collective-permute-start.11 = (bf16[64,4,1,1]{3,0,1,2:T(8,128)(2,1)S(1)}, bf16[64,4,1,1]{3,0,1,2:T(8,128)(2,1)S(1)}, u32[]{:S(2)}, u32[]{:S(2)}) collective-permute-start(bf16[64,4,1,1]{3,0,1,2:T(8,128)(2,1)S(1)} %get-tuple-element.96), channel_id=1, source_target_pairs={{1,0},{2,1},{3,2},{4,3},{5,4},{6,5},{7,6},{9,8},{10,9},{11,10},{12... | collective-permute-start | bytes 1544 | tf_op jit(solution)/shard_map/ppermute | solution.py:19
  127.7 9.2 %copy-start.9 = (bf16[32,4,2,256]{3,0,2,1:T(8,128)(2,1)}, bf16[32,4,2,256]{3,0,2,1:T(8,128)(2,1)S(1)}, u32[]{:S(2)}) copy-start(bf16[32,4,2,256]{3,0,2,1:T(8,128)(2,1)S(1)} %fusion.40) | copy-start | bytes 393220
  137.3 7.1 %copy-start.23 = (f32[8,32,64]{2,1,0:T(8,128)}, f32[8,32,64]{2,1,0:T(8,128)S(1)}, u32[]{:S(2)}) copy-start(f32[8,32,64]{2,1,0:T(8,128)S(1)} %fusion.113) | copy-start | bytes 196612
  138.2 19.3 %copy-start.21 = (f32[2,128,64]{1,2,0:T(8,128)S(1)}, f32[2,128,64]{1,2,0:T(8,128)}, u32[]{:S(2)}) copy-start(f32[2,128,64]{1,2,0:T(8,128)} %fusion.310) | copy-start | bytes 196612
  138.2 19.3 %copy-start.22 = (f32[2,128,64]{1,2,0:T(8,128)S(1)}, f32[2,128,64]{1,2,0:T(8,128)}, u32[]{:S(2)}) copy-start(f32[2,128,64]{1,2,0:T(8,128)} %convolution_add_fusion.31) | copy-start | bytes 196612
  138.8 13.4 %collective-permute-start.12 = (bf16[64,1,1,128]{3,0,1,2:T(8,128)(2,1)S(1)}, bf16[64,1,1,128]{3,0,1,2:T(8,128)(2,1)S(1)}, u32[]{:S(2)}, u32[]{:S(2)}) collective-permute-start(bf16[64,1,1,128]{3,0,1,2:T(8,128)(2,1)S(1)} %get-tuple-element.99), channel_id=1, source_target_pairs={{0,8},{8,16},{16,24},{1,9},{9,17},{17,25},{2,10},{10,18},{18,26},{... | collective-permute-start | bytes 49160 | tf_op jit(solution)/shard_map/ppermute | solution.py:17
  142.3 9.9 %collective-permute-start.13 = (bf16[64,1,1,128]{3,0,1,2:T(8,128)(2,1)S(1)}, bf16[64,1,1,128]{3,0,1,2:T(8,128)(2,1)S(1)}, u32[]{:S(2)}, u32[]{:S(2)}) collective-permute-start(bf16[64,1,1,128]{3,0,1,2:T(8,128)(2,1)S(1)} %get-tuple-element.100), channel_id=1, source_target_pairs={{8,0},{16,8},{24,16},{9,1},{17,9},{25,17},{10,2},{18,10},{26,18},{... | collective-permute-start | bytes 49160 | tf_op jit(solution)/shard_map/ppermute | solution.py:19
  144.4 14.0 %copy-start.2 = (f32[27,64,64]{2,1,0:T(8,128)}, f32[27,64,64]{2,1,0:T(8,128)S(1)}, u32[]{:S(2)}) copy-start(f32[27,64,64]{2,1,0:T(8,128)S(1)} %constant_dynamic-update-slice_fusion.3) | copy-start | bytes 1327108
  144.4 97.8 %all-to-all-start = ((bf16[8,2,3,4,2,128]{5,1,4,3,2,0:T(2,128)(2,1)}), bf16[8,2,3,4,2,128]{5,1,4,3,2,0:T(2,128)(2,1)S(1)}, u32[]{:S(2)}, u32[]{:S(2)}) async-start(bf16[8,2,3,4,2,128]{5,1,4,3,2,0:T(2,128)(2,1)} %broadcast_multiply_fusion), calls=%async_computation | async-start | bytes 196608 | tf_op jit(solution)/shard_map/all_to_all | solution.py:145
  152.1 161.2 %all-reduce.8.cloned.1.call-start = ((), (), s32[]{:S(2)}) async-start(), calls=%async_computation.1 | async-start | bytes 3178496 | tf_op jit(solution)/shard_map/psum | solution.py:197
  152.2 6.4 %copy-start.19 = (f32[2,128,64]{1,2,0:T(8,128)S(1)}, f32[2,128,64]{1,2,0:T(8,128)}, u32[]{:S(2)}) copy-start(f32[2,128,64]{1,2,0:T(8,128)} %fusion.308) | copy-start | bytes 196612
  152.3 4.5 %collective-permute-start.15 = (bf16[64,4,1,1]{3,0,1,2:T(8,128)(2,1)S(1)}, bf16[64,4,1,1]{3,0,1,2:T(8,128)(2,1)S(1)}, u32[]{:S(2)}, u32[]{:S(2)}) collective-permute-start(bf16[64,4,1,1]{3,0,1,2:T(8,128)(2,1)S(1)} %get-tuple-element.94), channel_id=1, source_target_pairs={{1,0},{2,1},{3,2},{4,3},{5,4},{6,5},{7,6},{9,8},{10,9},{11,10},{12... | collective-permute-start | bytes 1544 | tf_op jit(solution)/shard_map/ppermute | solution.py:19
  153.6 3.9 %collective-permute-start.14 = (bf16[64,4,1,1]{3,0,1,2:T(8,128)(2,1)S(1)}, bf16[64,4,1,1]{3,0,1,2:T(8,128)(2,1)S(1)}, u32[]{:S(2)}, u32[]{:S(2)}) collective-permute-start(bf16[64,4,1,1]{3,0,1,2:T(8,128)(2,1)S(1)} %get-tuple-element.93), channel_id=1, source_target_pairs={{0,1},{1,2},{2,3},{3,4},{4,5},{5,6},{6,7},{8,9},{9,10},{10,11},{11... | collective-permute-start | bytes 1544 | tf_op jit(solution)/shard_map/ppermute | solution.py:17
  166.9 6.6 %copy-start.44 = (bf16[32,4,2,256]{3,0,2,1:T(8,128)(2,1)S(1)}, bf16[32,4,2,256]{3,0,2,1:T(8,128)(2,1)}, u32[]{:S(2)}) copy-start(bf16[32,4,2,256]{3,0,2,1:T(8,128)(2,1)} %get-tuple-element.67) | copy-start | bytes 393220
  167.1 6.6 %copy-start.43 = (bf16[32,4,2,256]{3,0,2,1:T(8,128)(2,1)S(1)}, bf16[32,4,2,256]{3,0,2,1:T(8,128)(2,1)}, u32[]{:S(2)}) copy-start(bf16[32,4,2,256]{3,0,2,1:T(8,128)(2,1)} %get-tuple-element.51) | copy-start | bytes 393220
  167.3 6.6 %copy-start.42 = (bf16[32,4,2,256]{3,0,2,1:T(8,128)(2,1)S(1)}, bf16[32,4,2,256]{3,0,2,1:T(8,128)(2,1)}, u32[]{:S(2)}) copy-start(bf16[32,4,2,256]{3,0,2,1:T(8,128)(2,1)} %get-tuple-element.50) | copy-start | bytes 393220
  167.5 6.6 %copy-start.41 = (bf16[32,4,2,256]{3,0,2,1:T(8,128)(2,1)S(1)}, bf16[32,4,2,256]{3,0,2,1:T(8,128)(2,1)}, u32[]{:S(2)}) copy-start(bf16[32,4,2,256]{3,0,2,1:T(8,128)(2,1)} %get-tuple-element.49) | copy-start | bytes 393220
  167.6 6.6 %copy-start.26 = (bf16[32,2,1,128]{3,0,2,1:T(8,128)(2,1)S(1)}, bf16[32,2,1,128]{3,0,2,1:T(8,128)(2,1)}, u32[]{:S(2)}) copy-start(bf16[32,2,1,128]{3,0,2,1:T(8,128)(2,1)} %copy-done.25) | copy-start | bytes 49156
  167.8 7.3 %collective-permute-start.16 = (bf16[32,1,2,256]{3,0,2,1:T(8,128)(2,1)S(1)}, bf16[32,1,2,256]{3,0,2,1:T(8,128)(2,1)S(1)}, u32[]{:S(2)}, u32[]{:S(2)}) collective-permute-start(bf16[32,1,2,256]{3,0,2,1:T(8,128)(2,1)S(1)} %get-tuple-element.81), channel_id=1, source_target_pairs={{0,8},{8,16},{16,24},{1,9},{9,17},{17,25},{2,10},{10,18},{18,26},{... | collective-permute-start | bytes 98312 | tf_op jit(solution)/shard_map/ppermute | solution.py:17
  172.1 5.8 %collective-permute-start.17 = (bf16[32,1,2,256]{3,0,2,1:T(8,128)(2,1)S(1)}, bf16[32,1,2,256]{3,0,2,1:T(8,128)(2,1)S(1)}, u32[]{:S(2)}, u32[]{:S(2)}) collective-permute-start(bf16[32,1,2,256]{3,0,2,1:T(8,128)(2,1)S(1)} %get-tuple-element.82), channel_id=1, source_target_pairs={{8,0},{16,8},{24,16},{9,1},{17,9},{25,17},{10,2},{18,10},{26,18},{... | collective-permute-start | bytes 98312 | tf_op jit(solution)/shard_map/ppermute | solution.py:19
  178.0 4.1 %collective-permute-start.18 = (bf16[32,6,2,1]{3,0,2,1:T(8,128)(2,1)S(1)}, bf16[32,6,2,1]{3,0,2,1:T(8,128)(2,1)S(1)}, u32[]{:S(2)}, u32[]{:S(2)}) collective-permute-start(bf16[32,6,2,1]{3,0,2,1:T(8,128)(2,1)S(1)} %get-tuple-element.75), channel_id=1, source_target_pairs={{0,1},{1,2},{2,3},{3,4},{4,5},{5,6},{6,7},{8,9},{9,10},{10,11},{11... | collective-permute-start | bytes 2312 | tf_op jit(solution)/shard_map/ppermute | solution.py:17
  180.7 6.5 %collective-permute-start.19 = (bf16[32,6,2,1]{3,0,2,1:T(8,128)(2,1)S(1)}, bf16[32,6,2,1]{3,0,2,1:T(8,128)(2,1)S(1)}, u32[]{:S(2)}, u32[]{:S(2)}) collective-permute-start(bf16[32,6,2,1]{3,0,2,1:T(8,128)(2,1)S(1)} %get-tuple-element.76), channel_id=1, source_target_pairs={{1,0},{2,1},{3,2},{4,3},{5,4},{6,5},{7,6},{9,8},{10,9},{11,10},{12... | collective-permute-start | bytes 2312 | tf_op jit(solution)/shard_map/ppermute | solution.py:19
  195.9 46.4 %copy-start.96 = (s32[1,1,4]{2,1,0:T(1,128)S(1)}, s32[1,1,4]{2,1,0:T(1,128)}, u32[]{:S(2)}) copy-start(s32[1,1,4]{2,1,0:T(1,128)} %param.13) | copy-start | bytes 52
  195.9 46.4 %copy-start.97 = (pred[4]{0:T(512)(128)(4,1)S(1)}, pred[4]{0:T(512)(128)(4,1)}, u32[]{:S(2)}) copy-start(pred[4]{0:T(512)(128)(4,1)} %iota_compare_fusion.8) | copy-start | bytes 16
  (72 other events, 107.4 us)
Sparse Core Ops, SparseCore 0:
  175.2 138.1 all-reduce.7
where the time goes:
time: 327 us; the launch traced here: 325 us
  waiting for transfers between devices  94.4 us (29%)
  blocking collectives  80 us (24%)
  starting transfers between devices  54.6 us (17%)
  matrix products  41.6 us (13%)
  local copies, waits for them, and re-layouts  30.6 us (9%)
  between operations  16.7 us (5%)
  other arithmetic  7.44 us (2%)
    psum x1, waiting for transfers between devices, local(): lax.psum((grad_in, grad_res, grad_down, grad_mid, grad_up, head_weight_gr...  70.2 us
    psum x1, blocking collectives, local(): lax.psum((grad_in, grad_res, grad_down, grad_mid, grad_up, head_weight_gr...  44.9 us
    ppermute x10, starting transfers between devices, with_halo(): lax.ppermute(tail, axis, [(i, (i + 1) % count) for i in range(ends)])  33.7 us
    ppermute x10, waiting for transfers between devices, with_halo(): lax.ppermute(head, axis, [((i + 1) % count, i) for i in range(ends)])  23.5 us
    dot_general x108, matrix products, convolve(): jnp.einsum('oc,czyx->ozyx', weights[tap], window, preferred_element_type=...  22.8 us
    ppermute x10, starting transfers between devices, with_halo(): lax.ppermute(head, axis, [((i + 1) % count, i) for i in range(ends)])  13.1 us
    unnamed x226, local copies, waits for them, and re-layouts  12 us
    slice x16, local copies, waits for them, and re-layouts, strided(): return field[:, tap // 4::2, tap // 2 % 2::2, tap % 2::2]  11.8 us
  transfers between devices with their start and end apart: 22, of which 10 were waited for; matrix products, arithmetic and copies ran while one was open for 11% of the time, Pallas kernels for 0%

commit v1 on v0

--- a/solution.py
+++ b/solution.py
@@ -87,7 +87,26 @@
     )
     wanted = column * per_dev + jnp.arange(per_dev)
     piece_img = lax.all_gather(tile_image, "xy", axis=1, tiled=True)
-    piece_tgt = lax.all_gather(tile_target, "xy", axis=1, tiled=True)
+    count_2, index, rows = (lax.axis_size("xy"), lax.axis_index("xy"), tile_target.shape[1])
+    right = [(i_2, (i_2 + 1) % count_2) for i_2 in range(count_2)]
+    left = [(i_2, (i_2 - 1) % count_2) for i_2 in range(count_2)]
+    out = jnp.zeros(
+        (*tile_target.shape[:1], count_2 * rows, *tile_target.shape[1 + 1 :]), tile_target.dtype
+    )
+    out = lax.dynamic_update_slice_in_dim(out, tile_target, index * rows, axis=1)
+    from_left = from_right = tile_target
+    middle = count_2 // 2
+    for lap in range(1, middle + 1):
+        from_left = lax.ppermute(from_left, "xy", right)
+        out = lax.dynamic_update_slice_in_dim(
+            out, from_left, (index - lap) % count_2 * rows, axis=1
+        )
+        if lap < count_2 - middle:
+            from_right = lax.ppermute(from_right, "xy", left)
+            out = lax.dynamic_update_slice_in_dim(
+                out, from_right, (index + lap) % count_2 * rows, axis=1
+            )
+    piece_tgt = out
     piece_cnt = lax.all_gather(owner_counts, "xy", axis=1, tiled=True)
     piece_list = lax.all_gather(tile_list, "xy", axis=1, tiled=True)
     owners = piece_list.shape[1]

time: 327 us -> 339 us (1.037)
  local copies, waits for them, and re-layouts: 30.6 us -> 46.3 us
  starting transfers between devices: 54.6 us -> 64.1 us
  blocking collectives: 80 us -> 71.3 us
  waiting for transfers between devices: 94.4 us -> 88.6 us
    dynamic_update_slice x0 -> x8, local copies, waits for them, and re-layouts: none -> 14.2 us  [the longest x4 7.12 us: local(): lax.dynamic_update_slice_in_dim(out, from_left, (index - lap) % count_2 *...]
    ppermute x0 -> x7, starting transfers between devices: none -> 12.4 us  [the longest x4 8.89 us: local(): from_left = lax.ppermute(from_left, 'xy', right)]
    all_gather x1 -> x0, blocking collectives: 8.6 us -> none  [local(): piece_tgt = lax.all_gather(tile_target, 'xy', axis=1, tiled=True)]
    ppermute x10, waiting for transfers between devices: 23.5 us -> 17.5 us  [with_halo(): lax.ppermute(head, axis, [((i + 1) % count, i) for i in range(ends)])]
    unnamed x226 -> x235, local copies, waits for them, and re-layouts: 12 us -> 12.3 us
  transfers between devices with their start and end apart: 22 -> 29, of which waited for: 10 -> 7; matrix products, arithmetic and copies ran while one was open for 11% -> 22% of each run, Pallas kernels for 0% -> 0%
where the time goes in v1:
time: 339 us; the launch traced here: 337 us
  waiting for transfers between devices  88.6 us (26%)
  blocking collectives  71.3 us (21%)
  starting transfers between devices  64.1 us (19%)
  local copies, waits for them, and re-layouts  46.3 us (14%)
  matrix products  42.8 us (13%)
  between operations  17 us (5%)
  other arithmetic  7.49 us (2%)
    psum x1, waiting for transfers between devices, local(): lax.psum((grad_in, grad_res, grad_down, grad_mid, grad_up, head_weight_gr...  70.5 us
    psum x1, blocking collectives, local(): lax.psum((grad_in, grad_res, grad_down, grad_mid, grad_up, head_weight_gr...  46.2 us
    ppermute x10, starting transfers between devices, with_halo(): lax.ppermute(tail, axis, [(i, (i + 1) % count) for i in range(ends)])  33.1 us
    dot_general x108, matrix products, convolve(): jnp.einsum('oc,czyx->ozyx', weights[tap], window, preferred_element_type=...  24 us
    ppermute x10, waiting for transfers between devices, with_halo(): lax.ppermute(head, axis, [((i + 1) % count, i) for i in range(ends)])  17.5 us
    ppermute x10, starting transfers between devices, with_halo(): lax.ppermute(head, axis, [((i + 1) % count, i) for i in range(ends)])  13.4 us
    unnamed x235, local copies, waits for them, and re-layouts  12.3 us
    slice x16, local copies, waits for them, and re-layouts, strided(): return field[:, tap // 4::2, tap // 2 % 2::2, tap % 2::2]  11.8 us
  transfers between devices with their start and end apart: 29, of which 7 were waited for; matrix products, arithmetic and copies ran while one was open for 22% of the time, Pallas kernels for 0%

profile of v1, /device:TPU:0, one launch (start us, length us, event | category | flops | bytes accessed | tf_op | source)
XLA Modules:
  0.0 337.5 jit_solution(1718762251031828880)
XLA Ops:
  7.7 2.9 collective-permute-start.13
  13.3 8.1 %all-reduce.3 = s32[8]{0:T(128)S(1)} all-reduce(s32[8]{0:T(128)S(1)} %bitcast_dynamic-update-slice_fusion), channel_id=1, replica_groups=mesh['gz'=4,'xy'=8] {'xy'}, use_global_device_ids=true, to_apply=%add.3 | all-reduce | flops 8 | bytes 64
  21.4 8.5 %all_gather.9 = s32[1,8,4]{2,0,1:T(1,128)S(1)} all-gather(s32[1,1,4]{2,0,1:T(1,128)} %bitcast.2114), channel_id=1, replica_groups=mesh['gz'=4,'xy'=8] {'xy'}, dimensions={1}, use_global_device_ids=true | all-gather | bytes 144 | tf_op jit(solution)/shard_map/all_gather | solution.py:111
  30.6 8.6 %all_gather.11 = bf16[1,8,4,4,2,128]{5,3,4,2,0,1:T(4,128)(2,1)S(1)} all-gather(bf16[1,1,4,4,2,128]{5,3,4,2,0,1:T(4,128)(2,1)S(1)} %copy.249), channel_id=1, replica_groups=mesh['gz'=4,'xy'=8] {'xy'}, dimensions={1}, use_global_device_ids=true | all-gather | bytes 73728 | tf_op jit(solution)/shard_map/all_gather | solution.py:89
  39.5 3.5 %collective-permute-start = (bf16[1,1,2,256]{3,2,1,0:T(2,128)(2,1)S(1)}, bf16[1,1,2,256]{3,2,1,0:T(2,128)(2,1)S(1)}, u32[]{:S(2)}, u32[]{:S(2)}) collective-permute-start(bf16[1,1,2,256]{3,2,1,0:T(2,128)(2,1)S(1)} %get-tuple-element.194), channel_id=1, source_target_pairs={{0,8},{8,16},{16,24},{1,9},{9,17},{17,25},{2,10},{10,18},{18,26},{... | collective-permute-start | bytes 3080 | tf_op jit(solution)/shard_map/ppermute | solution.py:17
  43.0 1.3 collective-permute-start.1
  47.0 1.5 fusion.348
  48.5 1.5 fusion.338
  50.0 1.3 copy.266
  56.4 1.8 dynamic_update_slice.32
  59.0 2.0 collective-permute-start.2
  60.9 1.3 collective-permute-start.3
  62.2 2.5 collective-permute-done.3
  67.1 4.5 %collective-permute-start.4 = (bf16[32,1,2,256]{3,0,2,1:T(8,128)(2,1)S(1)}, bf16[32,1,2,256]{3,0,2,1:T(8,128)(2,1)S(1)}, u32[]{:S(2)}, u32[]{:S(2)}) collective-permute-start(bf16[32,1,2,256]{3,0,2,1:T(8,128)(2,1)S(1)} %get-tuple-element.91), channel_id=1, source_target_pairs={{0,8},{8,16},{16,24},{1,9},{9,17},{17,25},{2,10},{10,18},{18,26},{... | collective-permute-start | bytes 98312 | tf_op jit(solution)/shard_map/ppermute | solution.py:17
  71.6 1.3 collective-permute-start.5
  73.2 1.8 dynamic_update_slice.33
  75.0 1.8 dynamic_update_slice.34
  76.8 2.1 collective-permute-start.14
  79.6 1.8 collective-permute-start.6
  81.5 1.5 collective-permute-start.7
  83.6 2.5 collective-permute-done.7
  97.9 1.9 fusion.749
  102.6 4.3 %collective-permute-start.8 = (bf16[64,1,1,128]{3,0,1,2:T(8,128)(2,1)S(1)}, bf16[64,1,1,128]{3,0,1,2:T(8,128)(2,1)S(1)}, u32[]{:S(2)}, u32[]{:S(2)}) collective-permute-start(bf16[64,1,1,128]{3,0,1,2:T(8,128)(2,1)S(1)} %get-tuple-element.101), channel_id=1, source_target_pairs={{0,8},{8,16},{16,24},{1,9},{9,17},{17,25},{2,10},{10,18},{18,26},{... | collective-permute-start | bytes 49160 | tf_op jit(solution)/shard_map/ppermute | solution.py:17
  106.9 1.3 collective-permute-start.9
  109.9 1.8 dynamic_update_slice.35
  111.6 1.8 dynamic_update_slice.36
  113.4 3.0 collective-permute-start.16
  116.6 2.5 collective-permute-start.10
  119.1 1.3 collective-permute-start.11
  120.6 4.9 %collective-permute-done.11 = bf16[64,4,1,1]{3,0,1,2:T(8,128)(2,1)S(1)} collective-permute-done((bf16[64,4,1,1]{3,0,1,2:T(8,128)(2,1)S(1)}, bf16[64,4,1,1]{3,0,1,2:T(8,128)(2,1)S(1)}, u32[]{:S(2)}, u32[]{:S(2)}) %collective-permute-start.11) | collective-permute-done | bytes 544 | tf_op jit(solution)/shard_map/ppermute | solution.py:19
  130.2 3.2 collective-permute-start.18
  133.7 1.8 dynamic_update_slice.37
  135.4 1.8 dynamic_update_slice.38
  137.3 1.8 dynamic_update_slice.39
  150.8 4.3 %collective-permute-start.19 = (bf16[64,1,1,128]{3,0,1,2:T(8,128)(2,1)S(1)}, bf16[64,1,1,128]{3,0,1,2:T(8,128)(2,1)S(1)}, u32[]{:S(2)}, u32[]{:S(2)}) collective-permute-start(bf16[64,1,1,128]{3,0,1,2:T(8,128)(2,1)S(1)} %get-tuple-element.99), channel_id=1, source_target_pairs={{0,8},{8,16},{16,24},{1,9},{9,17},{17,25},{2,10},{10,18},{18,26},{... | collective-permute-start | bytes 49160 | tf_op jit(solution)/shard_map/ppermute | solution.py:17
  155.1 1.3 collective-permute-start.20
  157.2 5.2 %all-to-all-start = ((bf16[8,2,3,4,2,128]{5,1,4,3,2,0:T(2,128)(2,1)}), bf16[8,2,3,4,2,128]{5,1,4,3,2,0:T(2,128)(2,1)S(1)}, u32[]{:S(2)}, u32[]{:S(2)}) async-start(bf16[8,2,3,4,2,128]{5,1,4,3,2,0:T(2,128)(2,1)} %broadcast_multiply_fusion), calls=%async_computation | async-start | bytes 196608 | tf_op jit(solution)/shard_map/all_to_all | solution.py:164
  162.6 1.3 collective-permute-start.22
  163.9 3.0 collective-permute-start.21
  178.1 4.6 %collective-permute-start.23 = (bf16[32,1,2,256]{3,0,2,1:T(8,128)(2,1)S(1)}, bf16[32,1,2,256]{3,0,2,1:T(8,128)(2,1)S(1)}, u32[]{:S(2)}, u32[]{:S(2)}) collective-permute-start(bf16[32,1,2,256]{3,0,2,1:T(8,128)(2,1)S(1)} %get-tuple-element.81), channel_id=1, source_target_pairs={{0,8},{8,16},{16,24},{1,9},{9,17},{17,25},{2,10},{10,18},{18,26},{... | collective-permute-start | bytes 98312 | tf_op jit(solution)/shard_map/ppermute | solution.py:17
  185.7 2.8 collective-permute-done.24
  188.6 2.6 collective-permute-start.25
  191.2 1.6 collective-permute-start.26
  193.0 4.8 %collective-permute-done.26 = bf16[32,6,2,1]{3,0,2,1:T(8,128)(2,1)S(1)} collective-permute-done((bf16[32,6,2,1]{3,0,2,1:T(8,128)(2,1)S(1)}, bf16[32,6,2,1]{3,0,2,1:T(8,128)(2,1)S(1)}, u32[]{:S(2)}, u32[]{:S(2)}) %collective-permute-start.26) | collective-permute-done | bytes 800 | tf_op jit(solution)/shard_map/ppermute | solution.py:19
  208.0 46.2 %all-reduce.4 = (f32[27,32]{1,0:T(8,128)}, f32[3,32]{1,0:T(4,128)}) all-reduce(f32[27,32]{1,0:T(8,128)S(1)} %bitcast.2099, f32[3,32]{1,0:T(4,128)S(1)} %copy-done.100), channel_id=1, replica_groups=mesh['gz'=4,'xy'=8] {'gz','xy'}, use_global_device_ids=true, to_apply=%region_1.2 | all-reduce | flops 960 | bytes 7680 | tf_op jit(solution)/shard_map/psum | solution.py:216
  255.1 70.5 %all-reduce.8.cloned.1.call-done = (f32[27,32,32]{2,1,0:T(8,128)}, f32[8,64,32]{1,2,0:T(8,128)}, f32[27,64,64]{2,1,0:T(8,128)}, f32[8,32,64]{2,1,0:T(8,128)}) async-done(((f32[27,32,32]{2,1,0:T(8,128)}, f32[8,64,32]{1,2,0:T(8,128)}, f32[27,64,64]{2,1,0:T(8,128)}, f32[8,32,64]{2,1,0:T(8,128)}), (f32[27,32,32]{2,1,0:T(8,128)}, f32[8,64,32]{1,2,0:T(8,128)}, f32[27,64,64]{2,1,0:T(8,128)}, ...) | async-done | bytes 684048 | tf_op jit(solution)/shard_map/psum | solution.py:216
  325.6 1.9 copy.840
  327.4 1.6 copy.841
  (567 shorter events, 75.8 us)
Async XLA Ops:
  7.2 126.3 %copy-start = (bf16[3,32]{1,0:T(4,128)(2,1)S(1)}, bf16[3,32]{1,0:T(4,128)(2,1)}, u32[]{:S(2)}) copy-start(bf16[3,32]{1,0:T(4,128)(2,1)} %param.19) | copy-start | bytes 580
  7.2 65.9 %collective-permute-start.12 = (bf16[1,1,4,3,4,2,128]{6,5,4,3,2,1,0:T(2,128)(2,1)}, bf16[1,1,4,3,4,2,128]{6,5,4,3,2,1,0:T(2,128)(2,1)S(1)}, u32[]{:S(2)}, u32[]{:S(2)}) collective-permute-start(bf16[1,1,4,3,4,2,128]{6,5,4,3,2,1,0:T(2,128)(2,1)} %param.11), channel_id=1, source_target_pairs={{0,1},{1,2},{2,3},{3,4},{4,5},{5,6},{6,7},{7,0},{8,9},{9,10},{10,1... | collective-permute-start | bytes 73736 | tf_op jit(solution)/shard_map/ppermute | solution.py:100
  7.7 65.4 %collective-permute-start.13 = (bf16[1,1,4,3,4,2,128]{6,5,4,3,2,1,0:T(2,128)(2,1)}, bf16[1,1,4,3,4,2,128]{6,5,4,3,2,1,0:T(2,128)(2,1)S(1)}, u32[]{:S(2)}, u32[]{:S(2)}) collective-permute-start(bf16[1,1,4,3,4,2,128]{6,5,4,3,2,1,0:T(2,128)(2,1)} %param.11), channel_id=1, source_target_pairs={{0,7},{1,0},{2,1},{3,2},{4,3},{5,4},{6,5},{7,6},{8,15},{9,8},{10,9... | collective-permute-start | bytes 73736 | tf_op jit(solution)/shard_map/ppermute | solution.py:105
  13.3 39.8 %copy-start.96 = (s32[2]{0:T(128)}, s32[2]{0:T(128)S(1)}, u32[]{:S(2)}) copy-start(s32[2]{0:T(128)S(1)} %iota_add_fusion) | copy-start | bytes 28
  21.4 31.6 %copy-start.98 = (pred[8,4]{0,1:T(4,128)(4,1)}, pred[8,4]{0,1:T(4,128)(4,1)S(1)}, u32[]{:S(2)}) copy-start(pred[8,4]{0,1:T(4,128)(4,1)S(1)} %iota_compare_fusion.6) | copy-start | bytes 100
  39.5 18.8 %collective-permute-start = (bf16[1,1,2,256]{3,2,1,0:T(2,128)(2,1)S(1)}, bf16[1,1,2,256]{3,2,1,0:T(2,128)(2,1)S(1)}, u32[]{:S(2)}, u32[]{:S(2)}) collective-permute-start(bf16[1,1,2,256]{3,2,1,0:T(2,128)(2,1)S(1)} %get-tuple-element.194), channel_id=1, source_target_pairs={{0,8},{8,16},{16,24},{1,9},{9,17},{17,25},{2,10},{10,18},{18,26},{... | collective-permute-start | bytes 3080 | tf_op jit(solution)/shard_map/ppermute | solution.py:17
  43.0 15.3 %collective-permute-start.1 = (bf16[1,1,2,256]{3,2,1,0:T(2,128)(2,1)S(1)}, bf16[1,1,2,256]{3,2,1,0:T(2,128)(2,1)S(1)}, u32[]{:S(2)}, u32[]{:S(2)}) collective-permute-start(bf16[1,1,2,256]{3,2,1,0:T(2,128)(2,1)S(1)} %get-tuple-element.193), channel_id=1, source_target_pairs={{8,0},{16,8},{24,16},{9,1},{17,9},{25,17},{10,2},{18,10},{26,18},{... | collective-permute-start | bytes 3080 | tf_op jit(solution)/shard_map/ppermute | solution.py:19
  59.0 3.3 collective-permute-start.2
  60.9 3.8 %collective-permute-start.3 = (bf16[1,6,2,1]{3,2,1,0:T(2,128)(2,1)S(1)}, bf16[1,6,2,1]{3,2,1,0:T(2,128)(2,1)S(1)}, u32[]{:S(2)}, u32[]{:S(2)}) collective-permute-start(bf16[1,6,2,1]{3,2,1,0:T(2,128)(2,1)S(1)} %get-tuple-element.185), channel_id=1, source_target_pairs={{1,0},{2,1},{3,2},{4,3},{5,4},{6,5},{7,6},{9,8},{10,9},{11,10},{12... | collective-permute-start | bytes 80 | tf_op jit(solution)/shard_map/ppermute | solution.py:19
  67.1 12.4 %collective-permute-start.4 = (bf16[32,1,2,256]{3,0,2,1:T(8,128)(2,1)S(1)}, bf16[32,1,2,256]{3,0,2,1:T(8,128)(2,1)S(1)}, u32[]{:S(2)}, u32[]{:S(2)}) collective-permute-start(bf16[32,1,2,256]{3,0,2,1:T(8,128)(2,1)S(1)} %get-tuple-element.91), channel_id=1, source_target_pairs={{0,8},{8,16},{16,24},{1,9},{9,17},{17,25},{2,10},{10,18},{18,26},{... | collective-permute-start | bytes 98312 | tf_op jit(solution)/shard_map/ppermute | solution.py:17
  71.6 7.9 %collective-permute-start.5 = (bf16[32,1,2,256]{3,0,2,1:T(8,128)(2,1)S(1)}, bf16[32,1,2,256]{3,0,2,1:T(8,128)(2,1)S(1)}, u32[]{:S(2)}, u32[]{:S(2)}) collective-permute-start(bf16[32,1,2,256]{3,0,2,1:T(8,128)(2,1)S(1)} %get-tuple-element.92), channel_id=1, source_target_pairs={{8,0},{16,8},{24,16},{9,1},{17,9},{25,17},{10,2},{18,10},{26,18},{... | collective-permute-start | bytes 98312 | tf_op jit(solution)/shard_map/ppermute | solution.py:19
  76.8 31.5 %collective-permute-start.14 = (bf16[1,1,4,3,4,2,128]{6,5,4,3,2,1,0:T(2,128)(2,1)S(1)}, bf16[1,1,4,3,4,2,128]{6,5,4,3,2,1,0:T(2,128)(2,1)}, u32[]{:S(2)}, u32[]{:S(2)}) collective-permute-start(bf16[1,1,4,3,4,2,128]{6,5,4,3,2,1,0:T(2,128)(2,1)S(1)} %collective-permute-done.12), channel_id=1, source_target_pairs={{0,1},{1,2},{2,3},{3,4},{4,5},{5,6},{6,7},{7,0},{8,9},{9,10},{10,1... | collective-permute-start | bytes 73736 | tf_op jit(solution)/shard_map/ppermute | solution.py:100
  78.9 30.2 %collective-permute-start.15 = (bf16[1,1,4,3,4,2,128]{6,5,4,3,2,1,0:T(2,128)(2,1)S(1)}, bf16[1,1,4,3,4,2,128]{6,5,4,3,2,1,0:T(2,128)(2,1)}, u32[]{:S(2)}, u32[]{:S(2)}) collective-permute-start(bf16[1,1,4,3,4,2,128]{6,5,4,3,2,1,0:T(2,128)(2,1)S(1)} %collective-permute-done.13), channel_id=1, source_target_pairs={{0,7},{1,0},{2,1},{3,2},{4,3},{5,4},{6,5},{7,6},{8,15},{9,8},{10,9... | collective-permute-start | bytes 73736 | tf_op jit(solution)/shard_map/ppermute | solution.py:105
  79.6 3.6 %collective-permute-start.6 = (bf16[32,6,2,1]{3,0,2,1:T(8,128)(2,1)S(1)}, bf16[32,6,2,1]{3,0,2,1:T(8,128)(2,1)S(1)}, u32[]{:S(2)}, u32[]{:S(2)}) collective-permute-start(bf16[32,6,2,1]{3,0,2,1:T(8,128)(2,1)S(1)} %get-tuple-element.79), channel_id=1, source_target_pairs={{0,1},{1,2},{2,3},{3,4},{4,5},{5,6},{6,7},{8,9},{9,10},{10,11},{11... | collective-permute-start | bytes 2312 | tf_op jit(solution)/shard_map/ppermute | solution.py:17
  81.5 4.7 %collective-permute-start.7 = (bf16[32,6,2,1]{3,0,2,1:T(8,128)(2,1)S(1)}, bf16[32,6,2,1]{3,0,2,1:T(8,128)(2,1)S(1)}, u32[]{:S(2)}, u32[]{:S(2)}) collective-permute-start(bf16[32,6,2,1]{3,0,2,1:T(8,128)(2,1)S(1)} %get-tuple-element.80), channel_id=1, source_target_pairs={{1,0},{2,1},{3,2},{4,3},{5,4},{6,5},{7,6},{9,8},{10,9},{11,10},{12... | collective-permute-start | bytes 2312 | tf_op jit(solution)/shard_map/ppermute | solution.py:19
  83.0 8.1 %copy-start.5 = (bf16[32,4,2,256]{3,0,2,1:T(8,128)(2,1)}, bf16[32,4,2,256]{3,0,2,1:T(8,128)(2,1)S(1)}, u32[]{:S(2)}) copy-start(bf16[32,4,2,256]{3,0,2,1:T(8,128)(2,1)S(1)} %get-tuple-element.89) | copy-start | bytes 393220
  92.6 8.2 %copy-start.41 = (bf16[32,2,1,128]{3,0,2,1:T(8,128)(2,1)}, bf16[32,2,1,128]{3,0,2,1:T(8,128)(2,1)S(1)}, u32[]{:S(2)}) copy-start(bf16[32,2,1,128]{3,0,2,1:T(8,128)(2,1)S(1)} %slice.1254) | copy-start | bytes 49156
  93.4 7.7 %copy-start.39 = (bf16[32,2,1,128]{3,0,2,1:T(8,128)(2,1)}, bf16[32,2,1,128]{3,0,2,1:T(8,128)(2,1)S(1)}, u32[]{:S(2)}) copy-start(bf16[32,2,1,128]{3,0,2,1:T(8,128)(2,1)S(1)} %slice.1256) | copy-start | bytes 49156
  94.1 7.1 %copy-start.37 = (bf16[32,2,1,128]{3,0,2,1:T(8,128)(2,1)}, bf16[32,2,1,128]{3,0,2,1:T(8,128)(2,1)S(1)}, u32[]{:S(2)}) copy-start(bf16[32,2,1,128]{3,0,2,1:T(8,128)(2,1)S(1)} %slice.1258) | copy-start | bytes 49156
  101.9 23.9 %copy-start.21 = (f32[2,128,64]{1,2,0:T(8,128)S(1)}, f32[2,128,64]{1,2,0:T(8,128)}, u32[]{:S(2)}) copy-start(f32[2,128,64]{1,2,0:T(8,128)} %fusion.348) | copy-start | bytes 196612
  101.9 23.9 %copy-start.22 = (f32[2,128,64]{1,2,0:T(8,128)S(1)}, f32[2,128,64]{1,2,0:T(8,128)}, u32[]{:S(2)}) copy-start(f32[2,128,64]{1,2,0:T(8,128)} %convolution_add_fusion.42) | copy-start | bytes 196612
  102.6 13.9 %collective-permute-start.8 = (bf16[64,1,1,128]{3,0,1,2:T(8,128)(2,1)S(1)}, bf16[64,1,1,128]{3,0,1,2:T(8,128)(2,1)S(1)}, u32[]{:S(2)}, u32[]{:S(2)}) collective-permute-start(bf16[64,1,1,128]{3,0,1,2:T(8,128)(2,1)S(1)} %get-tuple-element.101), channel_id=1, source_target_pairs={{0,8},{8,16},{16,24},{1,9},{9,17},{17,25},{2,10},{10,18},{18,26},{... | collective-permute-start | bytes 49160 | tf_op jit(solution)/shard_map/ppermute | solution.py:17
  106.9 9.6 %collective-permute-start.9 = (bf16[64,1,1,128]{3,0,1,2:T(8,128)(2,1)S(1)}, bf16[64,1,1,128]{3,0,1,2:T(8,128)(2,1)S(1)}, u32[]{:S(2)}, u32[]{:S(2)}) collective-permute-start(bf16[64,1,1,128]{3,0,1,2:T(8,128)(2,1)S(1)} %get-tuple-element.102), channel_id=1, source_target_pairs={{8,0},{16,8},{24,16},{9,1},{17,9},{25,17},{10,2},{18,10},{26,18},{... | collective-permute-start | bytes 49160 | tf_op jit(solution)/shard_map/ppermute | solution.py:19
  113.4 16.8 %collective-permute-start.16 = (bf16[1,1,4,3,4,2,128]{6,5,4,3,2,1,0:T(2,128)(2,1)}, bf16[1,1,4,3,4,2,128]{6,5,4,3,2,1,0:T(2,128)(2,1)S(1)}, u32[]{:S(2)}, u32[]{:S(2)}) collective-permute-start(bf16[1,1,4,3,4,2,128]{6,5,4,3,2,1,0:T(2,128)(2,1)} %collective-permute-done.14), channel_id=1, source_target_pairs={{0,1},{1,2},{2,3},{3,4},{4,5},{5,6},{6,7},{7,0},{8,9},{9,10},{10,1... | collective-permute-start | bytes 73736 | tf_op jit(solution)/shard_map/ppermute | solution.py:100
  116.4 17.2 %collective-permute-start.17 = (bf16[1,1,4,3,4,2,128]{6,5,4,3,2,1,0:T(2,128)(2,1)}, bf16[1,1,4,3,4,2,128]{6,5,4,3,2,1,0:T(2,128)(2,1)S(1)}, u32[]{:S(2)}, u32[]{:S(2)}) collective-permute-start(bf16[1,1,4,3,4,2,128]{6,5,4,3,2,1,0:T(2,128)(2,1)} %collective-permute-done.15), channel_id=1, source_target_pairs={{0,7},{1,0},{2,1},{3,2},{4,3},{5,4},{6,5},{7,6},{8,15},{9,8},{10,9... | collective-permute-start | bytes 73736 | tf_op jit(solution)/shard_map/ppermute | solution.py:105
  116.6 10.1 %copy-start.20 = (f32[2,128,64]{1,2,0:T(8,128)S(1)}, f32[2,128,64]{1,2,0:T(8,128)}, u32[]{:S(2)}) copy-start(f32[2,128,64]{1,2,0:T(8,128)} %fusion.338) | copy-start | bytes 196612
  116.6 9.1 %collective-permute-start.10 = (bf16[64,4,1,1]{3,0,1,2:T(8,128)(2,1)S(1)}, bf16[64,4,1,1]{3,0,1,2:T(8,128)(2,1)S(1)}, u32[]{:S(2)}, u32[]{:S(2)}) collective-permute-start(bf16[64,4,1,1]{3,0,1,2:T(8,128)(2,1)S(1)} %get-tuple-element.95), channel_id=1, source_target_pairs={{0,1},{1,2},{2,3},{3,4},{4,5},{5,6},{6,7},{8,9},{9,10},{10,11},{11... | collective-permute-start | bytes 1544 | tf_op jit(solution)/shard_map/ppermute | solution.py:17
  119.1 6.3 %collective-permute-start.11 = (bf16[64,4,1,1]{3,0,1,2:T(8,128)(2,1)S(1)}, bf16[64,4,1,1]{3,0,1,2:T(8,128)(2,1)S(1)}, u32[]{:S(2)}, u32[]{:S(2)}) collective-permute-start(bf16[64,4,1,1]{3,0,1,2:T(8,128)(2,1)S(1)} %get-tuple-element.96), channel_id=1, source_target_pairs={{1,0},{2,1},{3,2},{4,3},{5,4},{6,5},{7,6},{9,8},{10,9},{11,10},{12... | collective-permute-start | bytes 1544 | tf_op jit(solution)/shard_map/ppermute | solution.py:19
  129.8 9.2 %copy-start.97 = (s32[2]{0:T(128)S(1)}, s32[2]{0:T(128)}, u32[]{:S(2)}) copy-start(s32[2]{0:T(128)} %copy-done.96) | copy-start | bytes 28
  129.8 9.2 %copy-start.99 = (pred[8,4]{0,1:T(4,128)(4,1)S(1)}, pred[8,4]{0,1:T(4,128)(4,1)}, u32[]{:S(2)}) copy-start(pred[8,4]{0,1:T(4,128)(4,1)} %copy-done.98) | copy-start | bytes 100
  130.2 7.0 %collective-permute-start.18 = (bf16[1,1,4,3,4,2,128]{6,5,4,3,2,1,0:T(2,128)(2,1)S(1)}, bf16[1,1,4,3,4,2,128]{6,5,4,3,2,1,0:T(2,128)(2,1)S(1)}, u32[]{:S(2)}, u32[]{:S(2)}) collective-permute-start(bf16[1,1,4,3,4,2,128]{6,5,4,3,2,1,0:T(2,128)(2,1)S(1)} %collective-permute-done.16), channel_id=1, source_target_pairs={{0,1},{1,2},{2,3},{3,4},{4,5},{5,6},{6,7},{7,0},{8,9},{9,10},{10,1... | collective-permute-start | bytes 73736 | tf_op jit(solution)/shard_map/ppermute | solution.py:100
  139.7 9.2 %copy-start.9 = (bf16[32,4,2,256]{3,0,2,1:T(8,128)(2,1)}, bf16[32,4,2,256]{3,0,2,1:T(8,128)(2,1)S(1)}, u32[]{:S(2)}) copy-start(bf16[32,4,2,256]{3,0,2,1:T(8,128)(2,1)S(1)} %fusion.40) | copy-start | bytes 393220
  149.3 7.9 %copy-start.25 = (f32[8,32,64]{2,1,0:T(8,128)}, f32[8,32,64]{2,1,0:T(8,128)S(1)}, u32[]{:S(2)}) copy-start(f32[8,32,64]{2,1,0:T(8,128)S(1)} %fusion.113) | copy-start | bytes 196612
  150.3 17.6 %copy-start.23 = (f32[2,128,64]{1,2,0:T(8,128)S(1)}, f32[2,128,64]{1,2,0:T(8,128)}, u32[]{:S(2)}) copy-start(f32[2,128,64]{1,2,0:T(8,128)} %fusion.308) | copy-start | bytes 196612
  150.3 17.6 %copy-start.24 = (f32[2,128,64]{1,2,0:T(8,128)S(1)}, f32[2,128,64]{1,2,0:T(8,128)}, u32[]{:S(2)}) copy-start(f32[2,128,64]{1,2,0:T(8,128)} %convolution_add_fusion.31) | copy-start | bytes 196612
  150.8 11.7 %collective-permute-start.19 = (bf16[64,1,1,128]{3,0,1,2:T(8,128)(2,1)S(1)}, bf16[64,1,1,128]{3,0,1,2:T(8,128)(2,1)S(1)}, u32[]{:S(2)}, u32[]{:S(2)}) collective-permute-start(bf16[64,1,1,128]{3,0,1,2:T(8,128)(2,1)S(1)} %get-tuple-element.99), channel_id=1, source_target_pairs={{0,8},{8,16},{16,24},{1,9},{9,17},{17,25},{2,10},{10,18},{18,26},{... | collective-permute-start | bytes 49160 | tf_op jit(solution)/shard_map/ppermute | solution.py:17
  155.1 7.4 %collective-permute-start.20 = (bf16[64,1,1,128]{3,0,1,2:T(8,128)(2,1)S(1)}, bf16[64,1,1,128]{3,0,1,2:T(8,128)(2,1)S(1)}, u32[]{:S(2)}, u32[]{:S(2)}) collective-permute-start(bf16[64,1,1,128]{3,0,1,2:T(8,128)(2,1)S(1)} %get-tuple-element.100), channel_id=1, source_target_pairs={{8,0},{16,8},{24,16},{9,1},{17,9},{25,17},{10,2},{18,10},{26,18},{... | collective-permute-start | bytes 49160 | tf_op jit(solution)/shard_map/ppermute | solution.py:19
  157.2 11.4 %copy-start.2 = (f32[27,64,64]{2,1,0:T(8,128)}, f32[27,64,64]{2,1,0:T(8,128)S(1)}, u32[]{:S(2)}) copy-start(f32[27,64,64]{2,1,0:T(8,128)S(1)} %constant_dynamic-update-slice_fusion.3) | copy-start | bytes 1327108
  157.2 96.9 %all-to-all-start = ((bf16[8,2,3,4,2,128]{5,1,4,3,2,0:T(2,128)(2,1)}), bf16[8,2,3,4,2,128]{5,1,4,3,2,0:T(2,128)(2,1)S(1)}, u32[]{:S(2)}, u32[]{:S(2)}) async-start(bf16[8,2,3,4,2,128]{5,1,4,3,2,0:T(2,128)(2,1)} %broadcast_multiply_fusion), calls=%async_computation | async-start | bytes 196608 | tf_op jit(solution)/shard_map/all_to_all | solution.py:164
  162.4 163.1 %all-reduce.8.cloned.1.call-start = ((), (), s32[]{:S(2)}) async-start(), calls=%async_computation.1 | async-start | bytes 3178496 | tf_op jit(solution)/shard_map/psum | solution.py:216
  162.6 4.5 %collective-permute-start.22 = (bf16[64,4,1,1]{3,0,1,2:T(8,128)(2,1)S(1)}, bf16[64,4,1,1]{3,0,1,2:T(8,128)(2,1)S(1)}, u32[]{:S(2)}, u32[]{:S(2)}) collective-permute-start(bf16[64,4,1,1]{3,0,1,2:T(8,128)(2,1)S(1)} %get-tuple-element.94), channel_id=1, source_target_pairs={{1,0},{2,1},{3,2},{4,3},{5,4},{6,5},{7,6},{9,8},{10,9},{11,10},{12... | collective-permute-start | bytes 1544 | tf_op jit(solution)/shard_map/ppermute | solution.py:19
  163.9 3.9 %collective-permute-start.21 = (bf16[64,4,1,1]{3,0,1,2:T(8,128)(2,1)S(1)}, bf16[64,4,1,1]{3,0,1,2:T(8,128)(2,1)S(1)}, u32[]{:S(2)}, u32[]{:S(2)}) collective-permute-start(bf16[64,4,1,1]{3,0,1,2:T(8,128)(2,1)S(1)} %get-tuple-element.93), channel_id=1, source_target_pairs={{0,1},{1,2},{2,3},{3,4},{4,5},{5,6},{6,7},{8,9},{9,10},{10,11},{11... | collective-permute-start | bytes 1544 | tf_op jit(solution)/shard_map/ppermute | solution.py:17
  178.1 7.6 %collective-permute-start.23 = (bf16[32,1,2,256]{3,0,2,1:T(8,128)(2,1)S(1)}, bf16[32,1,2,256]{3,0,2,1:T(8,128)(2,1)S(1)}, u32[]{:S(2)}, u32[]{:S(2)}) collective-permute-start(bf16[32,1,2,256]{3,0,2,1:T(8,128)(2,1)S(1)} %get-tuple-element.81), channel_id=1, source_target_pairs={{0,8},{8,16},{16,24},{1,9},{9,17},{17,25},{2,10},{10,18},{18,26},{... | collective-permute-start | bytes 98312 | tf_op jit(solution)/shard_map/ppermute | solution.py:17
  182.7 5.8 %collective-permute-start.24 = (bf16[32,1,2,256]{3,0,2,1:T(8,128)(2,1)S(1)}, bf16[32,1,2,256]{3,0,2,1:T(8,128)(2,1)S(1)}, u32[]{:S(2)}, u32[]{:S(2)}) collective-permute-start(bf16[32,1,2,256]{3,0,2,1:T(8,128)(2,1)S(1)} %get-tuple-element.82), channel_id=1, source_target_pairs={{8,0},{16,8},{24,16},{9,1},{17,9},{25,17},{10,2},{18,10},{26,18},{... | collective-permute-start | bytes 98312 | tf_op jit(solution)/shard_map/ppermute | solution.py:19
  188.6 4.3 %collective-permute-start.25 = (bf16[32,6,2,1]{3,0,2,1:T(8,128)(2,1)S(1)}, bf16[32,6,2,1]{3,0,2,1:T(8,128)(2,1)S(1)}, u32[]{:S(2)}, u32[]{:S(2)}) collective-permute-start(bf16[32,6,2,1]{3,0,2,1:T(8,128)(2,1)S(1)} %get-tuple-element.75), channel_id=1, source_target_pairs={{0,1},{1,2},{2,3},{3,4},{4,5},{5,6},{6,7},{8,9},{9,10},{10,11},{11... | collective-permute-start | bytes 2312 | tf_op jit(solution)/shard_map/ppermute | solution.py:17
  191.2 6.5 %collective-permute-start.26 = (bf16[32,6,2,1]{3,0,2,1:T(8,128)(2,1)S(1)}, bf16[32,6,2,1]{3,0,2,1:T(8,128)(2,1)S(1)}, u32[]{:S(2)}, u32[]{:S(2)}) collective-permute-start(bf16[32,6,2,1]{3,0,2,1:T(8,128)(2,1)S(1)} %get-tuple-element.76), channel_id=1, source_target_pairs={{1,0},{2,1},{3,2},{4,3},{5,4},{6,5},{7,6},{9,8},{10,9},{11,10},{12... | collective-permute-start | bytes 2312 | tf_op jit(solution)/shard_map/ppermute | solution.py:19
  206.5 47.7 %copy-start.101 = (s32[1,1,4]{2,1,0:T(1,128)S(1)}, s32[1,1,4]{2,1,0:T(1,128)}, u32[]{:S(2)}) copy-start(s32[1,1,4]{2,1,0:T(1,128)} %param.13) | copy-start | bytes 52
  206.5 47.7 %copy-start.102 = (pred[4]{0:T(512)(128)(4,1)S(1)}, pred[4]{0:T(512)(128)(4,1)}, u32[]{:S(2)}) copy-start(pred[4]{0:T(512)(128)(4,1)} %iota_compare_fusion.8) | copy-start | bytes 16
  (84 other events, 179.9 us)
Sparse Core Ops, SparseCore 0:
  185.8 139.7 all-reduce.7
